TPU v7x, 256 devices: a whole 4x4x8 slice. The times are simulated.
256 devices in a mesh: row: 16 (over z_lo, x, core), col: 16 (over z_hi, y).
Axes of the slice: x: 4, y: 4, z: 8 (z_hi: 4, z_lo: 2; z = z_hi * 2 + z_lo), core: 2. Of those that a mesh axis runs over, the one named last changes fastest.
Arguments:
- features: bfloat16 [65536, 512], P(('col', 'row')), may hold values from -6 to 6
- weight: bfloat16 [512, 512], replicated, may hold values from -0.25 to 0.25
- entry_values: bfloat16 [16, 16, 32, 128, 128], P('row', 'col'), may hold values from 0.0009994507 to 0.019897461
- block_rows: int32 [16, 16, 32], P('row', 'col'), may hold values from 0 to 31
- block_cols: int32 [16, 16, 32], P('row', 'col'), may hold values from 0 to 31
- entry_counts: int32 [16, 16], P('row', 'col'), may hold values from 8 to 32, as said below
- cotangent: bfloat16 [65536, 512], P(('row', 'col')), may hold values from -1.5 to 1.5
Outputs:
- output: bfloat16 [65536, 512], P(('row', 'col'))
- grad_features: bfloat16 [65536, 512], P(('col', 'row'))
- grad_weight: float32 [512, 512], replicated
Inputs may be any that keep to these rules, and one draw needn't show every extreme that they name: `entry_counts`: each grid cell has at least 8 live slots; at least one cell has all 32 live.
All inputs are finite; a program needn't handle non-finite values.
Results may differ from a plain program's by a relative error of at most 0.022.
Values may be sent and summed in bfloat16 or wider, within the bound.
No kernel may reach another device: no remote copies, remote signals or barrier semaphores. Data moves between devices by JAX's collectives and lax.ppermute only.
A program may use at most 128 MiB of HBM per device.

v0:
```python
import jax
import jax.numpy as jnp
from jax import lax
from jax.sharding import PartitionSpec as P


def block_terms(values, source_ids, target_ids, live_count, source, target_blocks, transpose):
    entry_total = values.shape[0]
    block_side = values.shape[1]
    feature_count = source.shape[1]
    group_size = min(32, entry_total)
    source_tiles = source.reshape(-1, block_side, feature_count)

    def one_group(group_index, running):
        first_entry = group_index * group_size
        tiles = jnp.take(source_tiles, source_ids, axis=0)
        if transpose:
            products = jnp.einsum("kba,kbf->kaf", values, tiles, preferred_element_type=jnp.float32)
        else:
            products = jnp.einsum("kab,kbf->kaf", values, tiles, preferred_element_type=jnp.float32)
        alive_mask = (first_entry + jnp.arange(group_size) < live_count).astype(jnp.float32)
        return running.at[target_ids].add(products * alive_mask[:, None, None])

    zero_sum = jnp.zeros((target_blocks, block_side, feature_count), jnp.float32)
    trip_count = entry_total // group_size
    running = lax.fori_loop(0, trip_count, one_group, zero_sum)
    return running.reshape(target_blocks * block_side, feature_count)


def silu_slope(summed):
    sigmoid_value = jax.nn.sigmoid(summed)
    return sigmoid_value * (1.0 + summed * (1.0 - sigmoid_value))


def shards(features, weight, entry_values, block_rows, block_cols, entry_counts, cotangent):
    values = entry_values[0, 0]
    row_ids = block_rows[0, 0]
    col_ids = block_cols[0, 0]
    live_count = entry_counts[0, 0]
    local_rows = features.shape[0]
    block_side = values.shape[1]
    row_span = lax.axis_size("col") * local_rows
    col_span = lax.axis_size("row") * local_rows
    projected = jnp.dot(features, weight, preferred_element_type=jnp.float32).astype(jnp.bfloat16)
    panel = lax.all_gather(projected, "row", axis=0, tiled=True)
    forward_terms = block_terms(
        values, col_ids, row_ids, live_count, panel, row_span // block_side, False
    )
    summed = lax.psum(forward_terms.astype(jnp.bfloat16), "col").astype(jnp.float32)
    position = lax.axis_index("col") * local_rows
    own_sum = lax.dynamic_slice_in_dim(summed, position, local_rows, 0)
    output = jax.nn.silu(own_sum).astype(jnp.bfloat16)
    incoming = lax.all_gather(cotangent, "col", axis=0, tiled=True)
    upstream = (incoming.astype(jnp.float32) * silu_slope(summed)).astype(jnp.bfloat16)
    backward_terms = block_terms(
        values, row_ids, col_ids, live_count, upstream, col_span // block_side, True
    )
    grad_projected = lax.psum_scatter(
        backward_terms.astype(jnp.bfloat16), "row", scatter_dimension=0, tiled=True
    )
    weight_term = lax.dot_general(
        features, grad_projected, (((0,), (0,)), ((), ())), preferred_element_type=jnp.float32
    )
    grad_weight = lax.psum(weight_term, ("row", "col"))
    grad_features = lax.dot_general(
        grad_projected, weight, (((1,), (1,)), ((), ())), preferred_element_type=jnp.float32
    ).astype(jnp.bfloat16)
    return (output, grad_features, grad_weight)


def solution(mesh):
    placed = (
        P(("col", "row"), None),
        P(),
        P("row", "col", None, None, None),
        P("row", "col", None),
        P("row", "col", None),
        P("row", "col"),
        P(("row", "col"), None),
    )
    return jax.shard_map(
        shards,
        mesh=mesh,
        in_specs=placed,
        out_specs=(P(("row", "col"), None), P(("col", "row"), None), P()),
        check_vma=False,
    )
```

profile of v0, /device:TPU:2, one launch (start us, length us, event | category | flops | bytes accessed | tf_op | source)
XLA Modules:
  0.0 751.3 jit_solution(11538004060448155654)
XLA Ops:
  7.2 0.0 copy-start
  7.2 0.0 all-gather.3.cloned.1.call-start
  7.2 2.2 convolution_convert_fusion.1
  9.4 0.0 all-gather.3.cloned.1.call-update
  9.5 0.0 all-gather.5.cloned.1.call-start
  9.5 0.7 all-gather.5.cloned.1.call-update
  10.2 0.0 all-reduce.3.cloned.1.call-start
  10.9 0.7 compare_select_fusion.1
  11.6 0.7 fusion.14
  12.2 0.7 compare_and_fusion.1
  12.9 39.9 %all-gather.3.cloned.1.call-done = bf16[4096,512]{1,0:T(8,128)(2,1)} async-done(((bf16[256,512]{1,0:T(8,128)(2,1)}), bf16[4096,512]{1,0:T(8,128)(2,1)}) %all-gather.3.cloned.1.call-update) | async-done | bytes 4194320 | tf_op jit(solution)/shard_map/all_gather | solution.py:45
  52.8 5.0 gather_fusion
  57.8 0.0 copy-done
  57.8 7.1 multiply_bitcast_fusion.1
  64.9 9.1 %copy.14 = f32[32,128,512]{2,1,0:T(8,128)} copy(f32[32,128,512]{1,2,0:T(8,128)} %multiply_bitcast_fusion.1) | data formatting | bytes 16777216 | tf_op jit(solution)/shard_map/while/body/eval_jaxpr/mul | solution.py:22
  74.0 4.3 broadcast.57.clone
  78.2 18.3 %scatter_fusion = f32[32,128,512]{2,1,0:T(8,128)} fusion(f32[32,128,512]{2,1,0:T(8,128)} %broadcast.57.clone, s32[32]{0:T(128)S(1)} %fusion.14, f32[32,128,512]{2,1,0:T(8,128)} %copy.14), kind=kCustom, calls=%fused_computation.2 | custom fusion | flops 2097152 | bytes 25165952 | tf_op jit(solution)/shard_map/while/body/eval_jaxpr/scatter-add | solution.py:22
  96.5 0.0 copy-start.5
  96.5 0.0 copy-start.4
  96.5 6.0 convert_element_type.42
  102.5 0.0 all-reduce.3.cloned.1.call-update
  102.5 0.0 reduce-scatter.2.cloned.1.call-start
  102.6 0.0 copy-done.5
  102.6 0.0 copy-done.4
  102.6 28.0 %all-gather.5.cloned.1.call-done = bf16[4096,512]{1,0:T(8,128)(2,1)} async-done(((bf16[256,512]{1,0:T(8,128)(2,1)}), bf16[4096,512]{1,0:T(8,128)(2,1)}) %all-gather.5.cloned.1.call-update) | async-done | bytes 4194320 | tf_op jit(solution)/shard_map/all_gather | solution.py:53
  130.6 224.6 %all-reduce.3.cloned.1.call-done = bf16[4096,512]{1,0:T(8,128)(2,1)} async-done(((bf16[4096,512]{1,0:T(8,128)(2,1)}), bf16[4096,512]{1,0:T(8,128)(2,1)}) %all-reduce.3.cloned.1.call-update) | async-done | bytes 4194320 | tf_op jit(solution)/shard_map/psum | solution.py:49
  355.2 7.0 multiply_convert_fusion
  362.2 5.0 gather_fusion.1
  367.1 7.1 multiply_bitcast_fusion
  374.3 9.0 %copy.16 = f32[32,128,512]{2,1,0:T(8,128)} copy(f32[32,128,512]{1,2,0:T(8,128)} %multiply_bitcast_fusion) | data formatting | bytes 16777216 | tf_op jit(solution)/shard_map/while/body/eval_jaxpr/mul | solution.py:22
  383.3 4.3 broadcast.57
  387.6 18.3 %scatter_fusion.1 = f32[32,128,512]{2,1,0:T(8,128)} fusion(f32[32,128,512]{2,1,0:T(8,128)} %broadcast.57, s32[32]{0:T(128)S(1)} %fusion.15, f32[32,128,512]{2,1,0:T(8,128)} %copy.16), kind=kCustom, calls=%fused_computation.3 | custom fusion | flops 2097152 | bytes 25165952 | tf_op jit(solution)/shard_map/while/body/eval_jaxpr/scatter-add | solution.py:22
  405.9 6.0 convert_element_type.48
  411.9 0.0 reduce-scatter.2.cloned.1.call-update
  411.9 0.0 copy-start.1
  411.9 0.0 all-reduce.5.cloned.1.call-start
  412.0 63.4 %reduce-scatter.2.cloned.1.call-done = bf16[256,512]{1,0:T(8,128)(2,1)} async-done(((bf16[4096,512]{1,0:T(8,128)(2,1)}), bf16[256,512]{1,0:T(8,128)(2,1)}) %reduce-scatter.2.cloned.1.call-update) | async-done | bytes 262160 | tf_op jit(solution)/shard_map/reduce_scatter | solution.py:58
  475.4 0.0 copy-done.2
  475.4 0.0 copy-start.3
  475.4 2.3 convolution_bitcast_fusion
  477.7 0.0 all-reduce.5.cloned.1.call-update
  477.8 3.4 convert_element_type.44
  481.1 0.9 multiply_convert_fusion.1
  482.0 0.0 copy-done.1
  482.0 0.0 copy-done.3
  482.0 1.0 convolution_convert_fusion
  483.0 259.2 %all-reduce.5.cloned.1.call-done = f32[512,512]{0,1:T(8,128)} async-done(((f32[512,512]{0,1:T(8,128)}), f32[512,512]{0,1:T(8,128)}) %all-reduce.5.cloned.1.call-update) | async-done | bytes 1048592 | tf_op jit(solution)/shard_map/psum | solution.py:64
  742.2 2.5 copy.17
  (6 shorter events, 0.0 us)
Async XLA Ops:
  7.2 50.6 %copy-start = (bf16[1,1,32,128,128]{4,3,2,1,0:T(8,128)(2,1)S(1)}, bf16[1,1,32,128,128]{4,3,2,1,0:T(8,128)(2,1)}, u32[]{:S(2)}) copy-start(bf16[1,1,32,128,128]{4,3,2,1,0:T(8,128)(2,1)} %param.11) | copy-start | bytes 3145732
  7.2 45.6 %all-gather.3.cloned.1.call-start = ((), (), s32[]{:S(2)}) async-start(), calls=%async_computation.1 | async-start | bytes 4456448 | tf_op jit(solution)/shard_map/all_gather | solution.py:45
  9.5 121.2 %all-gather.5.cloned.1.call-start = ((), (), s32[]{:S(2)}) async-start(), calls=%async_computation.3 | async-start | bytes 4456448 | tf_op jit(solution)/shard_map/all_gather | solution.py:53
  10.2 345.0 %all-reduce.3.cloned.1.call-start = ((), (), s32[]{:S(2)}) async-start(), calls=%async_computation.2 | async-start | bytes 8388608 | tf_op jit(solution)/shard_map/psum | solution.py:49
  96.5 6.1 copy-start.5
  96.5 6.1 copy-start.4
  102.5 372.9 %reduce-scatter.2.cloned.1.call-start = ((), (), s32[]{:S(2)}) async-start(), calls=%async_computation.4 | async-start | bytes 4456448 | tf_op jit(solution)/shard_map/reduce_scatter | solution.py:58
  405.9 69.5 %copy-start.2 = (bf16[256,512]{1,0:T(8,128)(2,1)S(1)}, bf16[256,512]{1,0:T(8,128)(2,1)}, u32[]{:S(2)}) copy-start(bf16[256,512]{1,0:T(8,128)(2,1)} %param.9) | copy-start | bytes 786436
  411.9 70.1 %copy-start.1 = (bf16[512,512]{1,0:T(8,128)(2,1)S(1)}, bf16[512,512]{1,0:T(8,128)(2,1)}, u32[]{:S(2)}) copy-start(bf16[512,512]{1,0:T(8,128)(2,1)} %param.10) | copy-start | bytes 1572868
  411.9 330.3 %all-reduce.5.cloned.1.call-start = ((), (), s32[]{:S(2)}) async-start(), calls=%async_computation.5 | async-start | bytes 2097152 | tf_op jit(solution)/shard_map/psum | solution.py:64
  475.4 6.6 copy-start.3
Sparse Core Ops, SparseCore 0:
  10.4 42.3 all-gather.2
  55.2 75.3 all-gather.4
  133.3 221.8 all-reduce.2
  412.1 63.2 reduce-scatter.1
  481.3 260.9 all-reduce.4
where the time goes:
time: 752 us; the launch traced here: 751 us
  waiting for transfers between devices  616 us (82%)
  other arithmetic  61.8 us (8%)
  local copies, waits for them, and re-layouts  39.2 us (5%)
  matrix products  19.8 us (3%)
  between operations  14.5 us (2%)
    psum x1, waiting for transfers between devices, shards(): grad_weight = lax.psum(weight_term, ('row', 'col'))  259 us
    psum x1, waiting for transfers between devices, shards(): lax.psum(forward_terms.astype(jnp.bfloat16), 'col').astype(jnp.float32)  225 us
    reduce_scatter x1, waiting for transfers between devices, shards(): lax.psum_scatter(backward_terms.astype(jnp.bfloat16), 'row', scatter_dime...  63.4 us
    all_gather x1, waiting for transfers between devices, shards(): panel = lax.all_gather(projected, 'row', axis=0, tiled=True)  39.9 us
    scatter-add x2, other arithmetic, one_group(): return running.at[target_ids].add(products * alive_mask[:, None, None])  36.6 us
    all_gather x1, waiting for transfers between devices, shards(): incoming = lax.all_gather(cotangent, 'col', axis=0, tiled=True)  28 us
    mul x2, local copies, waits for them, and re-layouts, one_group(): return running.at[target_ids].add(products * alive_mask[:, None, None])  18.1 us
  transfers between devices with their start and end apart: 5, of which 5 were waited for; matrix products, arithmetic and copies ran while one was open for 8% of the time, Pallas kernels for 0%

commit v1 on v0

--- a/solution.py
+++ b/solution.py
@@ -42,7 +42,9 @@
     row_span = lax.axis_size("col") * local_rows
     col_span = lax.axis_size("row") * local_rows
     projected = jnp.dot(features, weight, preferred_element_type=jnp.float32).astype(jnp.bfloat16)
-    panel = lax.all_gather(projected, "row", axis=0, tiled=True)
+    panel = jnp.concatenate(
+        lax.all_to_all(jnp.stack([projected] * lax.axis_size("row")), "row", 0, 0), axis=0
+    )
     forward_terms = block_terms(
         values, col_ids, row_ids, live_count, panel, row_span // block_side, False
     )

time: 752 us -> 778 us (1.035)
  waiting for transfers between devices: 616 us -> 635 us
    all_to_all x0 -> x1, waiting for transfers between devices: none -> 83.8 us  [shards(): lax.all_to_all(jnp.stack([projected] * lax.axis_size('row')), 'row', 0, 0)]
    all_gather x1 -> x0, waiting for transfers between devices: 39.9 us -> none  [shards(): panel = lax.all_gather(projected, 'row', axis=0, tiled=True)]
    all_gather x1, waiting for transfers between devices: 28 us -> 0.02 us  [shards(): incoming = lax.all_gather(cotangent, 'col', axis=0, tiled=True)]
  transfers between devices with their start and end apart: 5 -> 5, of which waited for: 5 -> 4; matrix products, arithmetic and copies ran while one was open for 8% -> 7% of each run, Pallas kernels for 0% -> 0%
where the time goes in v1:
time: 778 us; the launch traced here: 777 us
  waiting for transfers between devices  635 us (82%)
  other arithmetic  59.9 us (8%)
  local copies, waits for them, and re-layouts  41.5 us (5%)
  matrix products  19.2 us (2%)
  between operations  14.6 us (2%)
    psum x1, waiting for transfers between devices, shards(): grad_weight = lax.psum(weight_term, ('row', 'col'))  259 us
    psum x1, waiting for transfers between devices, shards(): lax.psum(forward_terms.astype(jnp.bfloat16), 'col').astype(jnp.float32)  228 us
    all_to_all x1, waiting for transfers between devices, shards(): lax.all_to_all(jnp.stack([projected] * lax.axis_size('row')), 'row', 0, 0)  83.8 us
    reduce_scatter x1, waiting for transfers between devices, shards(): lax.psum_scatter(backward_terms.astype(jnp.bfloat16), 'row', scatter_dime...  63.6 us
    scatter-add x2, other arithmetic, one_group(): return running.at[target_ids].add(products * alive_mask[:, None, None])  36.7 us
    mul x2, local copies, waits for them, and re-layouts, one_group(): return running.at[target_ids].add(products * alive_mask[:, None, None])  18.1 us
  transfers between devices with their start and end apart: 5, of which 4 were waited for; matrix products, arithmetic and copies ran while one was open for 7% of the time, Pallas kernels for 0%

profile of v1, /device:TPU:2, one launch (start us, length us, event | category | flops | bytes accessed | tf_op | source)
XLA Modules:
  0.0 777.4 jit_solution(4520642364028519135)
XLA Ops:
  7.2 0.0 copy-start
  7.2 0.0 copy-start.4
  7.2 0.0 copy-start.5
  7.2 1.5 convolution_convert_fusion.1
  8.7 2.4 stack.2
  11.1 6.5 all-to-all-start
  17.6 0.0 all-gather.2.cloned.1.call-start
  17.7 0.7 all-gather.2.cloned.1.call-update
  18.3 0.0 all-reduce.3.cloned.1.call-start
  19.0 0.0 copy-done.4
  19.1 0.0 copy-done.5
  19.1 83.8 %all-to-all-done = bf16[16,256,512]{2,1,0:T(8,128)(2,1)} async-done(((bf16[16,256,512]{2,1,0:T(8,128)(2,1)}), bf16[16,256,512]{2,1,0:T(8,128)(2,1)}, u32[]{:S(2)}, u32[]{:S(2)}) %all-to-all-start) | async-done | bytes 4194336 | tf_op jit(solution)/shard_map/all_to_all | solution.py:46
  102.9 5.0 gather_fusion
  107.8 0.0 copy-done
  107.8 7.2 multiply_bitcast_fusion.1
  115.1 9.0 %copy.14 = f32[32,128,512]{2,1,0:T(8,128)} copy(f32[32,128,512]{1,2,0:T(8,128)} %multiply_bitcast_fusion.1) | data formatting | bytes 16777216 | tf_op jit(solution)/shard_map/while/body/eval_jaxpr/mul | solution.py:22
  124.1 4.3 broadcast.59.clone
  128.4 18.4 %scatter_fusion = f32[32,128,512]{2,1,0:T(8,128)} fusion(f32[32,128,512]{2,1,0:T(8,128)} %broadcast.59.clone, s32[32]{0:T(128)S(1)} %fusion.14, f32[32,128,512]{2,1,0:T(8,128)} %copy.14), kind=kCustom, calls=%fused_computation.2 | custom fusion | flops 2097152 | bytes 25165952 | tf_op jit(solution)/shard_map/while/body/eval_jaxpr/scatter-add | solution.py:22
  146.8 6.0 convert_element_type.42
  152.7 0.0 all-reduce.3.cloned.1.call-update
  152.7 0.2 reduce-scatter.2.cloned.1.call-start
  153.0 0.0 all-gather.2.cloned.1.call-done
  153.1 227.9 %all-reduce.3.cloned.1.call-done = bf16[4096,512]{1,0:T(8,128)(2,1)} async-done(((bf16[4096,512]{1,0:T(8,128)(2,1)}), bf16[4096,512]{1,0:T(8,128)(2,1)}) %all-reduce.3.cloned.1.call-update) | async-done | bytes 4194320 | tf_op jit(solution)/shard_map/psum | solution.py:51
  381.0 7.0 multiply_convert_fusion
  388.0 5.0 gather_fusion.1
  392.9 7.1 multiply_bitcast_fusion
  400.1 9.0 %copy.16 = f32[32,128,512]{2,1,0:T(8,128)} copy(f32[32,128,512]{1,2,0:T(8,128)} %multiply_bitcast_fusion) | data formatting | bytes 16777216 | tf_op jit(solution)/shard_map/while/body/eval_jaxpr/mul | solution.py:22
  409.1 4.3 broadcast.59
  413.4 18.3 %scatter_fusion.1 = f32[32,128,512]{2,1,0:T(8,128)} fusion(f32[32,128,512]{2,1,0:T(8,128)} %broadcast.59, s32[32]{0:T(128)S(1)} %fusion.15, f32[32,128,512]{2,1,0:T(8,128)} %copy.16), kind=kCustom, calls=%fused_computation.3 | custom fusion | flops 2097152 | bytes 25165952 | tf_op jit(solution)/shard_map/while/body/eval_jaxpr/scatter-add | solution.py:22
  431.7 0.0 copy-start.2
  431.7 6.0 convert_element_type.48
  437.7 0.0 reduce-scatter.2.cloned.1.call-update
  437.7 0.0 copy-start.1
  437.7 0.0 all-reduce.5.cloned.1.call-start
  437.8 63.6 %reduce-scatter.2.cloned.1.call-done = bf16[256,512]{1,0:T(8,128)(2,1)} async-done(((bf16[4096,512]{1,0:T(8,128)(2,1)}), bf16[256,512]{1,0:T(8,128)(2,1)}) %reduce-scatter.2.cloned.1.call-update) | async-done | bytes 262160 | tf_op jit(solution)/shard_map/reduce_scatter | solution.py:60
  501.4 0.0 copy-done.2
  501.4 0.0 copy-start.3
  501.4 2.3 convolution_bitcast_fusion
  503.7 0.0 all-reduce.5.cloned.1.call-update
  503.8 3.4 convert_element_type.44
  507.2 0.9 multiply_convert_fusion.1
  508.0 0.0 copy-done.1
  508.0 0.0 copy-done.3
  508.0 1.0 convolution_convert_fusion
  509.1 259.2 %all-reduce.5.cloned.1.call-done = f32[512,512]{0,1:T(8,128)} async-done(((f32[512,512]{0,1:T(8,128)}), f32[512,512]{0,1:T(8,128)}) %all-reduce.5.cloned.1.call-update) | async-done | bytes 1048592 | tf_op jit(solution)/shard_map/psum | solution.py:66
  768.3 2.5 copy.17
  (8 shorter events, 0.0 us)
Async XLA Ops:
  7.2 100.7 %copy-start = (bf16[1,1,32,128,128]{4,3,2,1,0:T(8,128)(2,1)S(1)}, bf16[1,1,32,128,128]{4,3,2,1,0:T(8,128)(2,1)}, u32[]{:S(2)}) copy-start(bf16[1,1,32,128,128]{4,3,2,1,0:T(8,128)(2,1)} %param.11) | copy-start | bytes 3145732
  7.2 11.9 %copy-start.4 = (s32[1,1,32]{2,1,0:T(1,128)S(1)}, s32[1,1,32]{2,1,0:T(1,128)}, u32[]{:S(2)}) copy-start(s32[1,1,32]{2,1,0:T(1,128)} %param.13) | copy-start | bytes 388
  7.2 11.9 %copy-start.5 = (s32[1,1,32]{2,1,0:T(1,128)S(1)}, s32[1,1,32]{2,1,0:T(1,128)}, u32[]{:S(2)}) copy-start(s32[1,1,32]{2,1,0:T(1,128)} %param.12) | copy-start | bytes 388
  11.1 91.8 %all-to-all-start = ((bf16[16,256,512]{2,1,0:T(8,128)(2,1)}), bf16[16,256,512]{2,1,0:T(8,128)(2,1)}, u32[]{:S(2)}, u32[]{:S(2)}) async-start(bf16[16,256,512]{2,1,0:T(8,128)(2,1)} %stack.2), calls=%async_computation | async-start | bytes 8388608 | tf_op jit(solution)/shard_map/all_to_all | solution.py:46
  17.6 135.4 %all-gather.2.cloned.1.call-start = ((), (), s32[]{:S(2)}) async-start(), calls=%async_computation.3 | async-start | bytes 4456448 | tf_op jit(solution)/shard_map/all_gather | solution.py:55
  18.3 362.7 %all-reduce.3.cloned.1.call-start = ((), (), s32[]{:S(2)}) async-start(), calls=%async_computation.2 | async-start | bytes 8388608 | tf_op jit(solution)/shard_map/psum | solution.py:51
  152.7 348.7 %reduce-scatter.2.cloned.1.call-start = ((), (), s32[]{:S(2)}) async-start(), calls=%async_computation.4 | async-start | bytes 4456448 | tf_op jit(solution)/shard_map/reduce_scatter | solution.py:60
  431.7 69.7 %copy-start.2 = (bf16[256,512]{1,0:T(8,128)(2,1)S(1)}, bf16[256,512]{1,0:T(8,128)(2,1)}, u32[]{:S(2)}) copy-start(bf16[256,512]{1,0:T(8,128)(2,1)} %param.9) | copy-start | bytes 786436
  437.7 70.3 %copy-start.1 = (bf16[512,512]{1,0:T(8,128)(2,1)S(1)}, bf16[512,512]{1,0:T(8,128)(2,1)}, u32[]{:S(2)}) copy-start(bf16[512,512]{1,0:T(8,128)(2,1)} %param.10) | copy-start | bytes 1572868
  437.7 330.6 %all-reduce.5.cloned.1.call-start = ((), (), s32[]{:S(2)}) async-start(), calls=%async_computation.5 | async-start | bytes 2097152 | tf_op jit(solution)/shard_map/psum | solution.py:66
  501.4 6.6 copy-start.3
Sparse Core Ops, SparseCore 0:
  20.8 94.2 all-gather.1
  152.9 228.0 all-reduce.2
  437.9 63.5 reduce-scatter.1
  507.3 260.9 all-reduce.4
